TPU v7x, 512 devices: a whole 4x4x16 slice. The times are simulated.
512 devices in a mesh: tensor: 4 (over x), request: 128 (over z, y, core).
Axes of the slice: x: 4, y: 4, z: 16, core: 2. Of those that a mesh axis runs over, the one named last changes fastest.
Arguments:
- hidden: bfloat16 [1024, 2048], P('request'), may hold values from -6 to 6
- norm_gain: float32 [2048], replicated, may hold values from 0.1 to 1.9
- w_query: bfloat16 [2048, 2048], P(None, 'tensor'), may hold values from -0.125 to 0.125
- w_keyval: bfloat16 [2048, 512], P(None, 'tensor'), may hold values from -0.125 to 0.125
- w_output: bfloat16 [2048, 2048], P('tensor'), may hold values from -0.125 to 0.125
- node_cache: bfloat16 [128, 4, 512, 128], P('request', 'tensor'), may hold values from -300 to 300
- leaf_cache: bfloat16 [1024, 4, 128, 128], P('request', 'tensor'), may hold values from -300 to 300
- leaf_branch: int32 [1024], replicated, may hold values from 0 to 63
- branch_root: int32 [64], replicated, may hold values from 0 to 7
- root_owner: int32 [8], replicated, may hold values from 0 to 127, as said below
- branch_owner: int32 [64], replicated, may hold values from 1 to 126, as said below
- root_len: int32 [8], replicated, may hold values from 1 to 512, as said below
- branch_len: int32 [64], replicated, may hold values from 1 to 512, as said below
- leaf_len: int32 [1024], P('request'), may hold values from 0 to 127, as said below
Outputs:
- mixed: bfloat16 [1024, 2048], P('request', 'tensor')
- new_entries: bfloat16 [1024, 4, 128], P('request', 'tensor')
Inputs may be any that keep to these rules, and one draw needn't show every extreme that they name: The 8 entries of root_owner are all different slots. `branch_owner`: different from every entry of root_owner and from one another. `root_len`: some root has exactly 512 positions. `branch_len`: some branch has exactly 512 positions. `leaf_len`: some leaf has exactly 127 positions.
All inputs are finite; a program needn't handle non-finite values.
Results may differ from a plain program's by a relative error of at most 0.029.
Values may be sent and summed in bfloat16 or wider, within the bound.
No kernel may reach another device: no remote copies, remote signals or barrier semaphores. Data moves between devices by JAX's collectives and lax.ppermute only.
A program may use at most 128 MiB of HBM per device.

v0:
```python
import jax
import jax.numpy as jnp
from jax import lax
from jax.sharding import PartitionSpec as P

FLOOR = -1e30


def rotate(values_in, positions):
    half_dim = values_in.shape[-1] // 2
    inverse_freq = 10000.0 ** (
        -(jnp.arange(half_dim, dtype=jnp.float32) * 2.0 / values_in.shape[-1])
    )
    angles = positions.astype(jnp.float32)[..., None] * inverse_freq
    angles = jnp.concatenate([angles, angles], -1)
    turned = jnp.concatenate([-values_in[..., half_dim:], values_in[..., :half_dim]], -1)
    return values_in * jnp.cos(angles) + turned * jnp.sin(angles)


def soft_part(scores, usable, value_rows, pattern):
    scores = jnp.where(usable, scores, FLOOR)
    peak = jnp.max(scores, -1)
    weights = jnp.where(usable, jnp.exp(scores - peak[..., None]), 0.0).astype(jnp.bfloat16)
    summed = jnp.einsum(pattern, weights, value_rows, preferred_element_type=jnp.float32)
    weight_sum = jnp.sum(weights.astype(jnp.float32), -1)
    return (summed, weight_sum, peak)


def local(
    hidden,
    norm_gain,
    w_query,
    w_keyval,
    w_output,
    node_cache,
    leaf_cache,
    leaf_branch,
    branch_root,
    root_owner,
    branch_owner,
    root_len,
    branch_len,
    leaf_len,
):
    head_dim = w_keyval.shape[1] // 2
    local_leaves = hidden.shape[0]
    group = w_query.shape[1] // head_dim
    factor = head_dim ** (-0.5)
    device = lax.axis_index("request")
    offset = device * local_leaves
    widened = hidden.astype(jnp.float32)
    normed = (
        widened * lax.rsqrt(jnp.mean(widened * widened, -1, keepdims=True) + 1e-05) * norm_gain
    ).astype(jnp.bfloat16)
    branch_ids = jnp.arange(branch_root.shape[0], dtype=jnp.int32)
    root_ids = jnp.arange(root_owner.shape[0], dtype=jnp.int32)
    branch_hits = leaf_branch[:, None] == branch_ids[None, :]
    leaf_root = jnp.sum(jnp.where(branch_hits, branch_root[None, :], 0), 1)
    root_hits = leaf_root[:, None] == root_ids[None, :]
    prefix_all = jnp.sum(jnp.where(root_hits, root_len[None, :], 0), 1) + jnp.sum(
        jnp.where(branch_hits, branch_len[None, :], 0), 1
    )
    positions = lax.dynamic_slice_in_dim(prefix_all, offset, local_leaves) + leaf_len
    raw_query = jnp.dot(normed, w_query, preferred_element_type=jnp.float32).reshape(
        local_leaves, group, head_dim
    )
    queries = rotate(raw_query, positions[:, None]).astype(jnp.bfloat16)
    raw_entry = jnp.dot(normed, w_keyval, preferred_element_type=jnp.float32)
    new_entry = jnp.concatenate(
        [rotate(raw_entry[:, :head_dim], positions), raw_entry[:, head_dim:]], -1
    ).astype(jnp.bfloat16)
    leaf_rows = leaf_cache[:, 0]
    slot_index = jnp.arange(leaf_rows.shape[1], dtype=jnp.int32)
    appended = jnp.where(
        (slot_index[None, :] == leaf_len[:, None])[:, :, None], new_entry[:, None, :], leaf_rows
    )
    leaf_scores = (
        jnp.einsum(
            "lgd,lkd->lgk", queries, appended[:, :, :head_dim], preferred_element_type=jnp.float32
        )
        * factor
    )
    leaf_usable = (slot_index[None, :] <= leaf_len[:, None])[:, None, :]
    leaf_sum, leaf_weight, leaf_peak = soft_part(
        leaf_scores, leaf_usable, appended[:, :, head_dim:], "lgk,lkd->lgd"
    )
    everyone = lax.all_gather(
        queries.reshape(local_leaves, group * head_dim), "request", axis=0, tiled=True
    )
    total_leaves = everyone.shape[0]
    mine_all = jnp.any(branch_hits & (branch_owner == device)[None, :], 1) | jnp.any(
        root_hits & (root_owner == device)[None, :], 1
    )
    my_length = jnp.sum(jnp.where(root_owner == device, root_len, 0)) + jnp.sum(
        jnp.where(branch_owner == device, branch_len, 0)
    )
    node_rows = node_cache[0, 0]
    node_usable = jnp.arange(node_rows.shape[0], dtype=jnp.int32) < my_length
    block_rows = 128
    block_count = total_leaves // block_rows

    def owner_block(stacked_in):
        rows_query, rows_mine = stacked_in
        scores = (
            jnp.einsum(
                "ngd,kd->ngk",
                rows_query,
                node_rows[:, :head_dim],
                preferred_element_type=jnp.float32,
            )
            * factor
        )
        usable = rows_mine[:, None, None] & node_usable[None, None, :]
        return soft_part(scores, usable, node_rows[:, head_dim:], "ngk,kd->ngd")

    results = lax.map(
        owner_block,
        (
            everyone.reshape(block_count, block_rows, group, head_dim),
            mine_all.reshape(block_count, block_rows),
        ),
    )
    own_sum = results[0].reshape(total_leaves, group, head_dim)
    own_weight = results[1].reshape(total_leaves, group)
    own_peak = results[2].reshape(total_leaves, group)
    global_peak = lax.pmax(own_peak.astype(jnp.bfloat16), "request").astype(own_peak.dtype)
    scaled = jnp.exp(own_peak - global_peak)
    shared_sum, remote_weight = (
        lax.psum_scatter(
            (scaled[..., None] * own_sum).reshape(total_leaves, group * head_dim),
            "request",
            scatter_dimension=0,
            tiled=True,
        ),
        lax.psum_scatter(scaled * own_weight, "request", scatter_dimension=0, tiled=True),
    )
    remote_sum = shared_sum.reshape(local_leaves, group, head_dim)
    remote_peak = lax.dynamic_slice_in_dim(global_peak, offset, local_leaves)
    peak = jnp.maximum(remote_peak, leaf_peak)
    remote_scale = jnp.exp(remote_peak - peak)
    leaf_scale = jnp.exp(leaf_peak - peak)
    numerator = remote_scale[..., None] * remote_sum + leaf_scale[..., None] * leaf_sum
    denominator = remote_scale * remote_weight + leaf_scale * leaf_weight
    attended = (
        (numerator / denominator[..., None])
        .astype(jnp.bfloat16)
        .reshape(local_leaves, group * head_dim)
    )
    term = jnp.dot(attended, w_output, preferred_element_type=jnp.float32)
    mixed = lax.psum_scatter(term, "tensor", scatter_dimension=1, tiled=True).astype(jnp.bfloat16)
    return (mixed, new_entry[:, None, :])


def solution(mesh):
    in_specs = (
        P("request", None),
        P(),
        P(None, "tensor"),
        P(None, "tensor"),
        P("tensor", None),
        P("request", "tensor", None, None),
        P("request", "tensor", None, None),
        P(),
        P(),
        P(),
        P(),
        P(),
        P(),
        P("request"),
    )
    out_specs = (P("request", "tensor"), P("request", "tensor", None))
    return jax.shard_map(local, mesh=mesh, in_specs=in_specs, out_specs=out_specs, check_vma=False)
```

profile of v0, /device:TPU:8, one launch (start us, length us, event | category | flops | bytes accessed | tf_op | source)
XLA Modules:
  0.0 1273.9 jit_solution(6114707259069529670)
XLA Ops:
  7.3 1.0 fusion.20
  8.4 1.3 fusion.27
  9.7 2.1 fusion.29
  16.9 132.0 %all-gather.2.cloned.1.call-done = bf16[1024,512]{1,0:T(8,128)(2,1)} async-done(((bf16[8,512]{1,0:T(8,128)(2,1)}), bf16[1024,512]{1,0:T(8,128)(2,1)}) %all-gather.2.cloned.1.call-update) | async-done | bytes 1048592 | tf_op jit(solution)/shard_map/all_gather | solution.py:87
  148.9 3.9 reshape.275
  152.8 2.3 copy.55
  155.1 88.6 %while.15 = (s32[]{:T(128)}, f32[8,128,8,64]{1,0,3,2:T(8,128)}, f32[8,128,8]{1,2,0:T(8,128)}, f32[8,128,8]{1,2,0:T(8,128)}, pred[8,128]{1,0:T(8,128)(4,1)}, /*in...) while((s32[]{:T(128)}, f32[8,128,8,64]{1,0,3,2:T(8,128)}, ...), condition=%wide.region_11.12_spmd.clone, body=%wide.region_8.11_spmd.clone.sunk | while | flops 142146048 | bytes 7636981 | solution.py:116
  155.1 0.7 dynamic-slice_bitcast_fusion.2
  156.5 0.7 convert_reduce_fusion.3
  157.8 0.7 fusion.52
  158.5 7.7 dynamic_update_slice.19
  166.2 0.7 dynamic-slice_bitcast_fusion.2
  167.5 0.7 convert_reduce_fusion.3
  168.8 0.7 fusion.52
  169.5 7.7 dynamic_update_slice.19
  177.3 0.7 dynamic-slice_bitcast_fusion.2
  178.6 0.7 convert_reduce_fusion.3
  179.9 0.7 fusion.52
  180.6 7.7 dynamic_update_slice.19
  188.3 0.7 dynamic-slice_bitcast_fusion.2
  189.7 0.7 convert_reduce_fusion.3
  191.0 0.7 fusion.52
  191.7 7.7 dynamic_update_slice.19
  199.4 0.7 dynamic-slice_bitcast_fusion.2
  200.8 0.7 convert_reduce_fusion.3
  202.1 0.7 fusion.52
  202.8 7.7 dynamic_update_slice.19
  211.8 0.7 convert_reduce_fusion.3
  213.1 0.7 fusion.52
  213.9 7.7 dynamic_update_slice.19
  222.9 0.7 convert_reduce_fusion.3
  224.2 0.7 fusion.52
  224.9 7.7 dynamic_update_slice.19
  234.0 0.7 convert_reduce_fusion.3
  235.3 0.7 fusion.52
  236.0 7.7 dynamic_update_slice.19
  243.7 0.8 bitcast_convert_fusion
  244.5 489.9 %pmax.7 = bf16[1024,8]{0,1:T(8,128)(2,1)S(1)} all-reduce(bf16[1024,8]{0,1:T(8,128)(2,1)S(1)} %bitcast_convert_fusion), channel_id=1, replica_groups=mesh['tensor'=4,'request'=128] {'request'}, use_global_device_ids=true, to_apply=%region_12.13 | all-reduce | flops 8192 | bytes 32768 | tf_op jit(solution)/shard_map/pmax | solution.py:126
  734.4 0.8 bitcast_multiply_fusion.1
  735.2 3.4 bitcast_multiply_fusion
  738.6 2.9 copy.68
  741.7 0.8 copy-done.5
  743.6 1.3 dynamic-slice
  745.5 491.0 %all-reduce = f32[1024,8]{0,1:T(8,128)S(1)} all-reduce(f32[1024,8]{0,1:T(8,128)S(1)} %get-tuple-element.129), channel_id=3, replica_groups=mesh['tensor'=4,'request'=128] {'request'}, use_global_device_ids=true, to_apply=%region_15.16.clone | all-reduce | flops 8192 | bytes 65536
  1236.8 0.8 copy.69
  1238.1 1.0 fusion.42
  1239.9 26.2 %reduce-scatter.6.cloned.1.call-done = f32[8,512]{1,0:T(8,128)} async-done(((f32[8,2048]{1,0:T(8,128)}), f32[8,512]{1,0:T(8,128)}) %reduce-scatter.6.cloned.1.call-update) | async-done | bytes 16400 | tf_op jit(solution)/shard_map/reduce_scatter | solution.py:150
  1266.0 1.3 convert_element_type.60
  (112 shorter events, 18.7 us)
Async XLA Ops:
  7.2 1230.9 %copy-start = (bf16[512,2048]{1,0:T(8,128)(2,1)S(1)}, bf16[512,2048]{1,0:T(8,128)(2,1)}, u32[]{:S(2)}) copy-start(bf16[512,2048]{1,0:T(8,128)(2,1)} %param.20) | copy-start | bytes 6291460
  7.2 4.7 copy-start.7
  7.2 4.7 copy-start.13
  7.2 4.7 copy-start.10
  7.2 4.9 copy-start.8
  7.2 5.0 copy-start.9
  7.2 6.2 copy-start.6
  7.2 6.3 copy-start.11
  7.3 6.9 copy-start.12
  7.3 141.7 %all-gather.2.cloned.1.call-start = ((), (), s32[]{:S(2)}) async-start(), calls=%async_computation.2 | async-start | bytes 1056768 | tf_op jit(solution)/shard_map/all_gather | solution.py:87
  11.8 137.1 %copy-start.1 = (f32[8,8,64]{2,1,0:T(8,128)}, f32[8,8,64]{2,1,0:T(8,128)S(1)}, u32[]{:S(2)}) copy-start(f32[8,8,64]{2,1,0:T(8,128)S(1)} %reshape.266) | copy-start | bytes 49156
  12.5 136.4 %copy-start.3 = (f32[8,8,64]{2,1,0:T(8,128)}, f32[8,8,64]{2,1,0:T(8,128)S(1)}, u32[]{:S(2)}) copy-start(f32[8,8,64]{2,1,0:T(8,128)S(1)} %maximum_multiply_fusion) | copy-start | bytes 49156
  13.3 1223.4 %reduce-scatter.8.cloned.1.call-start = ((), (), s32[]{:S(2)}) async-start(), calls=%async_computation.4 | async-start | bytes 2113536
  741.5 0.9 copy-start.5
  741.5 1.5 copy-start.2
  741.5 1.5 copy-start.4
  741.5 524.5 %reduce-scatter.6.cloned.1.call-start = ((), (), s32[]{:S(2)}) async-start(), calls=%async_computation.3 | async-start | bytes 81920 | tf_op jit(solution)/shard_map/reduce_scatter | solution.py:150
Sparse Core Ops, SparseCore 0:
  13.5 135.4 all-gather.1
  741.7 260.9 reduce-scatter.7
  1239.3 26.7 reduce-scatter.5
where the time goes:
time: 1280 us; the launch traced here: 1270 us
  blocking collectives  981 us (77%)
  waiting for transfers between devices  158 us (12%)
  local copies, waits for them, and re-layouts  85.3 us (7%)
  other arithmetic  18.2 us (1%)
  between operations  15.9 us (1%)
  matrix products  15 us (1%)
    unnamed x1, blocking collectives  491 us
    pmax x1, blocking collectives, local(): lax.pmax(own_peak.astype(jnp.bfloat16), 'request').astype(own_peak.dtype)  490 us
    all_gather x1, waiting for transfers between devices, local(): lax.all_gather(queries.reshape(local_leaves, group * head_dim), 'request'...  132 us
    dynamic_update_slice x16, local copies, waits for them, and re-layouts, local(): lax.map(owner_block, (everyone.reshape(block_count, block_rows, group, he...  66.5 us
    reduce_scatter x1, waiting for transfers between devices, local(): lax.psum_scatter(term, 'tensor', scatter_dimension=1, tiled=True)  26.2 us
  transfers between devices with their start and end apart: 3, of which 2 were waited for; matrix products, arithmetic and copies ran while one was open for 0% of the time, Pallas kernels for 0%

commit v1 on v0

--- a/solution.py
+++ b/solution.py
@@ -1,9 +1,26 @@
+import functools
 import jax
 import jax.numpy as jnp
 from jax import lax
 from jax.sharding import PartitionSpec as P
 
 FLOOR = -1e30
+
+
+def update_points_up(original, bus_axis):
+    u_next = jnp.concatenate(
+        lax.all_to_all(
+            jnp.stack(tuple((original for _ in range(lax.axis_size(bus_axis))))),
+            bus_axis,
+            split_axis=0,
+            concat_axis=0,
+        ),
+        axis=0,
+    )
+    return u_next
+
+
+_see_widths = functools.partial(update_points_up, bus_axis="request")
 
 
 def rotate(values_in, positions):
@@ -84,9 +101,7 @@
     leaf_sum, leaf_weight, leaf_peak = soft_part(
         leaf_scores, leaf_usable, appended[:, :, head_dim:], "lgk,lkd->lgd"
     )
-    everyone = lax.all_gather(
-        queries.reshape(local_leaves, group * head_dim), "request", axis=0, tiled=True
-    )
+    everyone = _see_widths(queries.reshape(local_leaves, group * head_dim))
     total_leaves = everyone.shape[0]
     mine_all = jnp.any(branch_hits & (branch_owner == device)[None, :], 1) | jnp.any(
         root_hits & (root_owner == device)[None, :], 1

time: 1280 us -> 1210 us (0.945)
  waiting for transfers between devices: 158 us -> 76.9 us
  starting transfers between devices: 0.12 us -> 19.6 us
    all_gather x1 -> x0, waiting for transfers between devices: 132 us -> none  [local(): lax.all_gather(queries.reshape(local_leaves, group * head_dim), 'request'...]
    all_to_all x0 -> x1, waiting for transfers between devices: none -> 49.1 us  [update_points_up(): lax.all_to_all(jnp.stack(tuple((original for _ in range(lax.axis_size(bus...]
    all_to_all x0 -> x1, starting transfers between devices: none -> 19.5 us  [update_points_up(): lax.all_to_all(jnp.stack(tuple((original for _ in range(lax.axis_size(bus...]
where the time goes in v1:
time: 1210 us
  blocking collectives  978 us (81%)
  local copies, waits for them, and re-layouts  84.5 us (7%)
  waiting for transfers between devices  76.9 us (6%)
  starting transfers between devices  19.6 us (2%)
  other arithmetic  17.5 us (1%)
  between operations  16.1 us (1%)
  matrix products  15 us (1%)
    unnamed x1, blocking collectives  491 us
    pmax x1, blocking collectives, local(): lax.pmax(own_peak.astype(jnp.bfloat16), 'request').astype(own_peak.dtype)  487 us
    dynamic_update_slice x16, local copies, waits for them, and re-layouts, local(): lax.map(owner_block, (everyone.reshape(block_count, block_rows, group, he...  66.5 us
    all_to_all x1, waiting for transfers between devices, update_points_up(): lax.all_to_all(jnp.stack(tuple((original for _ in range(lax.axis_size(bus...  49.1 us
    reduce_scatter x1, waiting for transfers between devices, local(): lax.psum_scatter(term, 'tensor', scatter_dimension=1, tiled=True)  27.7 us
  transfers between devices with their start and end apart: 3, of which 2 were waited for; matrix products, arithmetic and copies ran while one was open for 0% of the time, Pallas kernels for 0%

profile of v1, /device:TPU:8, one launch (start us, length us, event | category | flops | bytes accessed | tf_op | source)
XLA Modules:
  0.0 1207.9 jit_solution(12266339730740072560)
XLA Ops:
  7.3 1.0 fusion.20
  8.3 1.3 fusion.27
  9.6 2.1 fusion.29
  12.6 1.1 stack.3
  13.7 19.5 %all-to-all-start = ((bf16[128,8,512]{2,1,0:T(8,128)(2,1)}), bf16[128,8,512]{2,1,0:T(8,128)(2,1)S(1)}, u32[]{:S(2)}, u32[]{:S(2)}) async-start(bf16[128,8,512]{2,1,0:T(8,128)(2,1)} %stack.3), calls=%async_computation | async-start | bytes 2097152 | tf_op jit(solution)/shard_map/all_to_all | solution.py:12
  36.6 49.1 %all-to-all-done = bf16[128,8,512]{2,1,0:T(8,128)(2,1)S(1)} async-done(((bf16[128,8,512]{2,1,0:T(8,128)(2,1)}), bf16[128,8,512]{2,1,0:T(8,128)(2,1)S(1)}, u32[]{:S(2)}, u32[]{:S(2)}) %all-to-all-start) | async-done | bytes 1048608 | tf_op jit(solution)/shard_map/all_to_all | solution.py:12
  85.8 2.1 reshape_reshape.3
  87.8 2.3 copy.50
  90.1 88.6 %while.15 = (s32[]{:T(128)}, f32[8,128,8,64]{1,0,3,2:T(8,128)}, f32[8,128,8]{1,2,0:T(8,128)}, f32[8,128,8]{1,2,0:T(8,128)}, pred[8,128]{1,0:T(8,128)(4,1)}, /*in...) while((s32[]{:T(128)}, f32[8,128,8,64]{1,0,3,2:T(8,128)}, ...), condition=%wide.region_11.12_spmd.clone, body=%wide.region_8.11_spmd.clone.sunk | while | flops 142146048 | bytes 7636981 | solution.py:131
  90.1 0.7 dynamic-slice_bitcast_fusion.2
  91.5 0.7 convert_reduce_fusion.3
  92.8 0.7 fusion.52
  93.5 7.7 dynamic_update_slice.19
  101.2 0.7 dynamic-slice_bitcast_fusion.2
  102.5 0.7 convert_reduce_fusion.3
  103.8 0.7 fusion.52
  104.5 7.7 dynamic_update_slice.19
  113.6 0.7 convert_reduce_fusion.3
  114.9 0.7 fusion.52
  115.6 7.7 dynamic_update_slice.19
  124.7 0.7 convert_reduce_fusion.3
  126.0 0.7 fusion.52
  126.7 7.7 dynamic_update_slice.19
  135.8 0.7 convert_reduce_fusion.3
  137.0 0.7 fusion.52
  137.8 7.7 dynamic_update_slice.19
  146.8 0.7 convert_reduce_fusion.3
  148.1 0.7 fusion.52
  148.8 7.7 dynamic_update_slice.19
  156.5 0.7 dynamic-slice_bitcast_fusion.2
  157.9 0.7 convert_reduce_fusion.3
  159.2 0.7 fusion.52
  159.9 7.7 dynamic_update_slice.19
  169.0 0.7 convert_reduce_fusion.3
  170.3 0.7 fusion.52
  171.0 7.7 dynamic_update_slice.19
  178.7 0.8 bitcast_convert_fusion
  179.4 487.1 %pmax.7 = bf16[1024,8]{0,1:T(8,128)(2,1)S(1)} all-reduce(bf16[1024,8]{0,1:T(8,128)(2,1)S(1)} %bitcast_convert_fusion), channel_id=1, replica_groups=mesh['tensor'=4,'request'=128] {'request'}, use_global_device_ids=true, to_apply=%region_12.13 | all-reduce | flops 8192 | bytes 32768 | tf_op jit(solution)/shard_map/pmax | solution.py:141
  666.6 0.8 bitcast_multiply_fusion.1
  667.4 3.4 bitcast_multiply_fusion
  670.7 2.9 copy.61
  673.8 0.8 copy-done.5
  675.7 1.3 dynamic-slice
  677.7 491.0 %all-reduce = f32[1024,8]{0,1:T(8,128)S(1)} all-reduce(f32[1024,8]{0,1:T(8,128)S(1)} %get-tuple-element.121), channel_id=3, replica_groups=mesh['tensor'=4,'request'=128] {'request'}, use_global_device_ids=true, to_apply=%region_15.16.clone | all-reduce | flops 8192 | bytes 65536
  1169.0 0.8 copy.62
  1170.3 1.0 fusion.42
  1172.1 27.7 %reduce-scatter.6.cloned.1.call-done = f32[8,512]{1,0:T(8,128)} async-done(((f32[8,2048]{1,0:T(8,128)}), f32[8,512]{1,0:T(8,128)}) %reduce-scatter.6.cloned.1.call-update) | async-done | bytes 16400 | tf_op jit(solution)/shard_map/reduce_scatter | solution.py:165
  1199.8 1.3 convert_element_type.61
  (112 shorter events, 19.3 us)
Async XLA Ops:
  7.2 1163.1 %copy-start = (bf16[512,2048]{1,0:T(8,128)(2,1)S(1)}, bf16[512,2048]{1,0:T(8,128)(2,1)}, u32[]{:S(2)}) copy-start(bf16[512,2048]{1,0:T(8,128)(2,1)} %param.20) | copy-start | bytes 6291460
  7.2 4.6 copy-start.7
  7.2 4.6 copy-start.13
  7.2 4.6 copy-start.10
  7.2 4.8 copy-start.8
  7.2 4.9 copy-start.9
  11.6 21.6 %copy-start.6 = (bf16[1,1,512,128]{3,2,1,0:T(8,128)(2,1)S(1)}, bf16[1,1,512,128]{3,2,1,0:T(8,128)(2,1)}, u32[]{:S(2)}) copy-start(bf16[1,1,512,128]{3,2,1,0:T(8,128)(2,1)} %param.21) | copy-start | bytes 393220
  11.7 21.8 %copy-start.11 = (s32[8]{0:T(128)S(1)}, s32[8]{0:T(128)}, u32[]{:S(2)}) copy-start(s32[8]{0:T(128)} %param.25) | copy-start | bytes 100
  11.7 22.4 %copy-start.12 = (s32[64]{0:T(128)S(1)}, s32[64]{0:T(128)}, u32[]{:S(2)}) copy-start(s32[64]{0:T(128)} %param.26) | copy-start | bytes 772
  11.7 1.9 copy-start.1
  12.4 1.2 copy-start.3
  13.7 72.1 %all-to-all-start = ((bf16[128,8,512]{2,1,0:T(8,128)(2,1)}), bf16[128,8,512]{2,1,0:T(8,128)(2,1)S(1)}, u32[]{:S(2)}, u32[]{:S(2)}) async-start(bf16[128,8,512]{2,1,0:T(8,128)(2,1)} %stack.3), calls=%async_computation | async-start | bytes 2097152 | tf_op jit(solution)/shard_map/all_to_all | solution.py:12
  33.2 1135.8 %reduce-scatter.8.cloned.1.call-start = ((), (), s32[]{:S(2)}) async-start(), calls=%async_computation.4 | async-start | bytes 2113536
  673.7 0.9 copy-start.5
  673.7 1.5 copy-start.2
  673.7 1.5 copy-start.4
  673.7 526.1 %reduce-scatter.6.cloned.1.call-start = ((), (), s32[]{:S(2)}) async-start(), calls=%async_computation.3 | async-start | bytes 81920 | tf_op jit(solution)/shard_map/reduce_scatter | solution.py:165
Sparse Core Ops, SparseCore 0:
  673.8 262.5 reduce-scatter.7
  1171.5 28.2 reduce-scatter.5
